TPU v7x, 256 devices: a whole 4x4x8 slice. The times are simulated.
256 devices in a mesh: section: 2 (over core), seq: 32 (over z, x), cfg: 4 (over y).
Axes of the slice: x: 4, y: 4, z: 8, core: 2. Of those that a mesh axis runs over, the one named last changes fastest.
Arguments:
- hidden_states: bfloat16 [4, 4, 512, 3072], P('cfg', None, 'seq'), may hold values from -250 to 250
- latent: float32 [2, 4, 512, 64], P('section', None, 'seq'), may hold values from -6 to 6
- stale_cache: bfloat16 [2, 4, 32, 2048, 128], P('section', 'cfg', 'seq'), may hold values from -140 to 140
- qkv_weight: bfloat16 [2, 3072, 3, 2048], P('section', None, None, 'cfg'), may hold values from -0.109375 to 0.109375
- out_weight: bfloat16 [2, 3072, 2048], P('section', 'seq', 'cfg'), may hold values from -0.125 to 0.125
- modulation: float32 [2, 6, 3072], P('section'), may hold values from -2.5 to 2.5
- out_modulation: float32 [2, 3072], replicated, may hold values from -2.5 to 2.5
- proj_weight: bfloat16 [3072, 64], replicated, may hold values from -0.109375 to 0.109375
- solver_coef: float32 [2, 3], P('section'), may hold values from 0.5 to 2
- video_len: int32 [2], replicated, may hold values from 911 to 1822, as said below
- text_len: int32 [4], replicated, may hold values from 1 to 226, as said below
- positions: int32 [3, 2, 4, 512], P(None, None, None, 'seq'), may hold values from 0 to 47
Outputs:
- new_latent: float32 [2, 4, 512, 64], P('section', None, 'seq')
- new_cache: bfloat16 [2, 4, 32, 2048, 128], P('section', 'cfg', 'seq')
Inputs may be any that keep to these rules, and one draw needn't show every extreme that they name: `video_len`: in every draw one request has exactly 1822 video tokens. `text_len`: in every draw some sequence has all 226 text tokens live.
All inputs are finite; a program needn't handle non-finite values.
Results may differ from a plain program's by a relative error of at most 0.02.
Values may be sent and summed in bfloat16 or wider, within the bound.
No kernel may reach another device: no remote copies, remote signals or barrier semaphores. Data moves between devices by JAX's collectives and lax.ppermute only.
A program may use at most 128 MiB of HBM per device.

v0:
```python
import math
import jax
import jax.numpy as jnp
from jax import lax
from jax.sharding import PartitionSpec as P

HD = 64
TEXT = 226


def from_behind(value, axis, steps):
    count = lax.axis_size(axis)
    pairs = [(source, (source + steps) % count) for source in range(count)]
    return lax.ppermute(value, axis, pairs)


def row_norm(values):
    centered = values - jnp.mean(values, axis=-1, keepdims=True)
    return centered * lax.rsqrt(jnp.mean(centered * centered, axis=-1, keepdims=True) + 1e-05)


def head_norm(values):
    centered = values - jnp.mean(values, axis=-1, keepdims=True)
    return centered * lax.rsqrt(jnp.mean(centered * centered, axis=-1, keepdims=True) + 1e-06)


def rope_angles(places, head_size):
    half_size = head_size // 2
    pairs_t = head_size // 8
    pairs_h = (half_size - pairs_t) // 2
    pair_index = jnp.arange(half_size)
    first_part = pair_index < pairs_t
    second_part = jnp.logical_and(pair_index >= pairs_t, pair_index < pairs_t + pairs_h)
    third_part = pair_index >= pairs_t + pairs_h
    local_index = jnp.where(
        first_part,
        pair_index,
        jnp.where(second_part, pair_index - pairs_t, pair_index - pairs_t - pairs_h),
    )
    axis_span = jnp.where(first_part, 2 * pairs_t, 2 * pairs_h)
    frequency = jnp.exp(
        -math.log(10000.0) * 2.0 * local_index.astype(jnp.float32) / axis_span.astype(jnp.float32)
    )
    angles = places[0][..., None] * first_part.astype(jnp.float32)
    angles = angles + places[1][..., None] * second_part.astype(jnp.float32)
    angles = angles + places[2][..., None] * third_part.astype(jnp.float32)
    return angles * frequency


def rotate(values, cos_table, sin_table):
    half_size = values.shape[-1] // 2
    first_half = values[..., :half_size]
    second_half = values[..., half_size:]
    return jnp.concatenate(
        [
            first_half * cos_table - second_half * sin_table,
            second_half * cos_table + first_half * sin_table,
        ],
        axis=-1,
    )


def per_device(
    hidden_states,
    latent,
    stale_cache,
    qkv_weight,
    out_weight,
    modulation,
    out_modulation,
    proj_weight,
    solver_coef,
    video_len,
    text_len,
    positions,
):
    section_id = lax.axis_index("section")
    shard_id = lax.axis_index("seq")
    seq_devices = lax.axis_size("seq")
    cfg_devices = lax.axis_size("cfg")
    patches = hidden_states.shape[1]
    patch_dev = hidden_states.shape[2]
    width = hidden_states.shape[3]
    patch_len = patch_dev * seq_devices
    total_len = patch_len * patches
    group_heads = qkv_weight.shape[3] // HD
    seq_count = cfg_devices
    qkv_full = qkv_weight[0].reshape(width, 3, group_heads, HD)
    out_full = lax.all_gather(out_weight[0], "seq", axis=0, tiled=True).reshape(
        width, group_heads, HD
    )
    mod_rows = modulation[0]
    stale_rows = stale_cache[0, 0, 0]
    my_sequence = shard_id // group_heads
    row_ids = jnp.arange(total_len)
    text_limit = lax.dynamic_index_in_dim(text_len, my_sequence, keepdims=False)
    video_limit = lax.dynamic_index_in_dim(video_len, my_sequence // 2, keepdims=False)
    live_keys = jnp.where(row_ids < TEXT, row_ids < text_limit, row_ids - TEXT < video_limit)
    key_patch = row_ids // patch_len
    use_fresh = key_patch[None, :] <= jnp.arange(patches)[:, None]
    scale_factor = HD ** (-0.5)
    row_place = (
        jnp.arange(patches)[:, None] * patch_len
        + shard_id * patch_dev
        + jnp.arange(patch_dev)[None, :]
    )
    text_rows = (row_place < TEXT)[:, :, None]
    shift_rows = jnp.where(text_rows, mod_rows[3], mod_rows[0])
    scale_rows = jnp.where(text_rows, mod_rows[4], mod_rows[1])
    gate_rows = jnp.where(text_rows, mod_rows[5], mod_rows[2])
    angles = rope_angles(positions.astype(jnp.float32), HD)
    angles = jnp.where(text_rows[None], 0.0, angles)
    angles = jnp.repeat(angles, 2, axis=0)[:, None]
    cos_table = jnp.cos(angles)
    sin_table = jnp.sin(angles)

    def run(hidden):
        normed = row_norm(hidden.astype(jnp.float32))
        mixed_rows = (normed * (1.0 + scale_rows) + shift_rows).astype(jnp.bfloat16)
        mixed_rows = lax.all_gather(mixed_rows, "cfg", axis=0, tiled=True)
        projected = jnp.einsum(
            "spqd,djge->sgjpqe", mixed_rows, qkv_full, preferred_element_type=jnp.float32
        )
        queries = rotate(head_norm(projected[:, :, 0]), cos_table, sin_table)
        key_part = rotate(head_norm(projected[:, :, 1]), cos_table, sin_table)
        stacked = jnp.stack([queries, key_part, projected[:, :, 2]], axis=2).astype(jnp.bfloat16)
        outgoing = stacked.reshape(seq_count * group_heads, 3, patches, patch_dev * HD)
        incoming = lax.all_to_all(outgoing, "seq", split_axis=0, concat_axis=3, tiled=True)
        incoming = incoming.reshape(3, patches, patch_len, HD)
        fresh_rows = jnp.concatenate([incoming[1], incoming[2]], axis=-1).reshape(total_len, 2 * HD)
        key_rows = jnp.where(use_fresh[:, :, None], fresh_rows[None], stale_rows[None])
        scores = (
            jnp.einsum(
                "pqe,pke->pqk", incoming[0], key_rows[..., :HD], preferred_element_type=jnp.float32
            )
            * scale_factor
        )
        scores = jnp.where(live_keys[None, None, :], scores, -jnp.inf)
        row_max = jnp.max(scores, axis=-1, keepdims=True)
        weights = jnp.exp(scores - row_max)
        row_sum = jnp.sum(weights, axis=-1, keepdims=True)
        combined = jnp.einsum(
            "pqk,pke->pqe",
            weights.astype(jnp.bfloat16),
            key_rows[..., HD:],
            preferred_element_type=jnp.float32,
        )
        attended = (combined / row_sum).astype(jnp.bfloat16)
        attended = attended.reshape(patches, seq_devices, patch_dev * HD)[None]
        returned = lax.all_to_all(attended, "seq", split_axis=2, concat_axis=0, tiled=True)
        returned = returned.reshape(seq_count, group_heads, patches, patch_dev, HD)
        update = lax.psum_scatter(
            jnp.einsum("sgpqe,dge->spqd", returned, out_full, preferred_element_type=jnp.float32),
            "cfg",
            scatter_dimension=0,
            tiled=True,
        )
        result = (hidden.astype(jnp.float32) + gate_rows * update).astype(jnp.bfloat16)
        return (result, fresh_rows)

    first_out, first_cache = run(hidden_states)
    received = from_behind(first_out, "section", 1)
    second_out, second_cache = run(received)
    key_cache = jnp.where(section_id == 0, first_cache, second_cache)
    normed = row_norm(second_out.astype(jnp.float32))
    normed_out = (normed * (1.0 + out_modulation[1]) + out_modulation[0]).astype(jnp.bfloat16)
    predicted = jnp.einsum(
        "spqd,do->spqo", normed_out, proj_weight, preferred_element_type=jnp.float32
    )
    predicted_all = lax.all_gather(predicted, ("section", "cfg"), axis=0, tiled=True)
    predicted_all = predicted_all[predicted_all.shape[0] - seq_count :]
    pair_rows = lax.dynamic_slice_in_dim(predicted_all, 2 * section_id, 2, 0)
    solver_row = solver_coef[0]
    guided = pair_rows[0] + solver_row[2] * (pair_rows[1] - pair_rows[0])
    new_latent = solver_row[0] * latent[0] + solver_row[1] * guided
    return (new_latent[None], key_cache[None, None, None])


def solution(mesh):
    return jax.shard_map(
        per_device,
        mesh=mesh,
        in_specs=(
            P("cfg", None, "seq", None),
            P("section", None, "seq", None),
            P("section", "cfg", "seq", None, None),
            P("section", None, None, "cfg"),
            P("section", "seq", "cfg"),
            P("section", None, None),
            P(),
            P(),
            P("section", None),
            P(),
            P(),
            P(None, None, None, "seq"),
        ),
        out_specs=(P("section", None, "seq", None), P("section", "cfg", "seq", None, None)),
        check_vma=False,
    )
```

profile of v0, /device:TPU:1, one launch (start us, length us, event | category | flops | bytes accessed | tf_op | source)
XLA Modules:
  0.0 396.4 jit_solution(5097558336061669999)
XLA Ops:
  14.1 12.7 %copy.39 = bf16[1,3072,3,512]{1,3,2,0:T(8,128)(2,1)} copy(bf16[1,3072,3,512]{3,1,2,0:T(8,128)(2,1)} %param.15) | data formatting | bytes 18874368 | tf_op args[3]
  27.2 19.9 %all-gather.6.cloned.1.call-done = bf16[4,4,16,3072]{3,2,1,0:T(8,128)(2,1)} async-done(((bf16[1,4,16,3072]{3,2,1,0:T(8,128)(2,1)}), bf16[4,4,16,3072]{3,2,1,0:T(8,128)(2,1)}) %all-gather.6.cloned.1.call-update) | async-done | bytes 1572880 | tf_op jit(solution)/shard_map/all_gather | solution.py:120
  47.1 8.1 %convolution_bitcast_fusion.3 = f32[4,8,3,4,16,64]{5,4,1,2,3,0:T(8,128)S(1)} fusion(bf16[3072,3,8,64,1,1]{0,3,2,1,5,4:T(8,128)(2,1)} %bitcast.167, bf16[4,4,16,3072]{3,2,1,0:T(8,128)(2,1)} %all-gather.6.cloned.1.call-done), kind=kOutput, calls=%fused_computation.19 | convolution fusion | flops 2415919104 | bytes 12582912 | tf_op jit(solution)/shard_map/spqd,djge->sgjpqe/dot_general | solution.py:121
  62.9 9.5 %all-to-all-start = ((bf16[32,3,4,1024]{3,2,1,0:T(4,128)(2,1)}), bf16[32,3,4,1024]{3,2,1,0:T(4,128)(2,1)S(1)}, u32[]{:S(2)}, u32[]{:S(2)}) async-start(bf16[32,3,4,1024]{3,2,1,0:T(4,128)(2,1)} %copy.44), calls=%async_computation | async-start | bytes 1572864 | tf_op jit(solution)/shard_map/all_to_all | solution.py:128
  77.9 15.6 %all-to-all-done = bf16[32,3,4,1024]{3,2,1,0:T(4,128)(2,1)S(1)} async-done(((bf16[32,3,4,1024]{3,2,1,0:T(4,128)(2,1)}), bf16[32,3,4,1024]{3,2,1,0:T(4,128)(2,1)S(1)}, u32[]{:S(2)}, u32[]{:S(2)}) %all-to-all-start) | async-done | bytes 786464 | tf_op jit(solution)/shard_map/all_to_all | solution.py:128
  96.6 2.5 fusion
  99.2 3.7 fusion.2
  102.9 4.0 %fusion.25 = bf16[4,512,64]{1,2,0:T(8,128)(2,1)S(1)} fusion(bf16[4,2048,128]{1,2,0:T(8,128)(2,1)S(1)} %broadcast_select_fusion.1, f32[4,512,2048]{2,1,0:T(8,128)S(1)} %get-tuple-element.49, f32[4,512]{1,0:T(4,128)S(1)} %get-tuple-element.48, pred[2048]{0:T(1024)(128)(4,1)S(1)} %fusion.78, f32[4,512]{1,0:T(4,128)S(1)} %fusion.2), kind=kOutput, calls=%fused_computation.58 | convolution fusion | flops 553910272 | bytes 18106368 | tf_op jit(solution)/shard_map/pqk,pke->pqe/dot_general | solution.py:142
  107.8 16.0 %all_to_all.60 = bf16[1,4,32,1024]{3,1,0,2:T(4,128)(2,1)S(1)} all-to-all(bf16[1,4,32,1024]{3,1,0,2:T(4,128)(2,1)S(1)} %copy.52), channel_id=1, replica_groups=mesh['section'=2,'seq'=32,'cfg'=4] {'seq'}, dimensions={2} | all-to-all | bytes 524288 | tf_op jit(solution)/shard_map/all_to_all | solution.py:150
  124.3 27.8 %all-gather.10.cloned.1.call-done = bf16[1,3072,512]{2,1,0:T(8,128)(2,1)} async-done(((bf16[1,96,512]{2,1,0:T(8,128)(2,1)}), bf16[1,3072,512]{2,1,0:T(8,128)(2,1)}) %all-gather.10.cloned.1.call-update) | async-done | bytes 3145744 | tf_op jit(solution)/shard_map/all_gather | solution.py:89
  152.0 4.6 %copy.54 = bf16[1,3072,512]{1,2,0:T(8,128)(2,1)} copy(bf16[1,3072,512]{2,1,0:T(8,128)(2,1)} %all-gather.10.cloned.1.call-done) | data formatting | bytes 6291456 | tf_op jit(solution)/shard_map/all_gather | solution.py:89
  156.7 4.5 %convolution_bitcast_fusion.1 = f32[4,4,16,3072]{3,2,1,0:T(8,128)} fusion(bf16[4,8,4,16,64]{4,3,2,1,0:T(8,128)(2,1)S(1)} %reshape.453, bf16[3072,8,64,1,1]{0,2,4,1,3:T(8,128)(2,1)} %bitcast.169), kind=kOutput, calls=%fused_computation.15 | convolution fusion | flops 805306368 | bytes 6553600 | tf_op jit(solution)/shard_map/sgpqe,dge->spqd/dot_general | solution.py:153
  161.3 41.5 %reduce-scatter.3.cloned.1.call-done = f32[1,4,16,3072]{3,2,1,0:T(8,128)} async-done(((f32[4,4,16,3072]{3,2,1,0:T(8,128)}), f32[1,4,16,3072]{3,2,1,0:T(8,128)}) %reduce-scatter.3.cloned.1.call-update) | async-done | bytes 786448 | tf_op jit(solution)/shard_map/reduce_scatter | solution.py:152
  207.9 28.5 %all-gather.8.cloned.1.call-done = bf16[4,4,16,3072]{3,2,1,0:T(8,128)(2,1)} async-done(((bf16[1,4,16,3072]{3,2,1,0:T(8,128)(2,1)}), bf16[4,4,16,3072]{3,2,1,0:T(8,128)(2,1)}) %all-gather.8.cloned.1.call-update) | async-done | bytes 1572880 | tf_op jit(solution)/shard_map/all_gather | solution.py:120
  236.4 8.1 %convolution_bitcast_fusion.2 = f32[4,8,3,4,16,64]{5,4,1,3,0,2:T(8,128)S(1)} fusion(bf16[3072,3,8,64,1,1]{0,3,2,5,4,1:T(8,128)(2,1)} %bitcast.168, bf16[4,4,16,3072]{3,2,1,0:T(8,128)(2,1)} %all-gather.8.cloned.1.call-done), kind=kOutput, calls=%fused_computation.18 | convolution fusion | flops 2415919104 | bytes 12582912 | tf_op jit(solution)/shard_map/spqd,djge->sgjpqe/dot_general | solution.py:121
  252.9 30.6 %all_to_all.61 = bf16[32,3,4,1024]{3,2,1,0:T(4,128)(2,1)S(1)} all-to-all(bf16[32,3,4,1024]{3,2,1,0:T(4,128)(2,1)S(1)} %copy.60), channel_id=1, replica_groups=mesh['section'=2,'seq'=32,'cfg'=4] {'seq'}, dimensions={0} | all-to-all | bytes 1572864 | tf_op jit(solution)/shard_map/all_to_all | solution.py:128
  291.1 2.5 fusion.1
  293.6 3.7 fusion.4
  297.3 4.7 %fusion.35 = bf16[4,512,64]{1,2,0:T(8,128)(2,1)} fusion(bf16[4,2048,128]{1,2,0:T(8,128)(2,1)S(1)} %broadcast_select_fusion, f32[4,512,2048]{2,1,0:T(8,128)S(1)} %get-tuple-element.51, f32[4,512]{1,0:T(4,128)S(1)} %get-tuple-element.50, pred[2048]{0:T(1024)(128)(4,1)S(1)} %fusion.78, f32[4,512]{1,0:T(4,128)S(1)} %fusion.4), kind=kOutput, calls=%fused_computation.60 | convolution fusion | flops 553910272 | bytes 18106368 | tf_op jit(solution)/shard_map/pqk,pke->pqe/dot_general | solution.py:142
  303.9 16.0 %all_to_all.62 = bf16[1,4,32,1024]{3,1,0,2:T(4,128)(2,1)S(1)} all-to-all(bf16[1,4,32,1024]{3,1,0,2:T(4,128)(2,1)S(1)} %copy.67), channel_id=1, replica_groups=mesh['section'=2,'seq'=32,'cfg'=4] {'seq'}, dimensions={2} | all-to-all | bytes 524288 | tf_op jit(solution)/shard_map/all_to_all | solution.py:150
  320.2 4.6 %convolution_bitcast_fusion = f32[4,4,16,3072]{3,2,1,0:T(8,128)} fusion(bf16[4,8,4,16,64]{4,3,2,1,0:T(8,128)(2,1)S(1)} %reshape.454, bf16[3072,8,64,1,1]{0,2,4,1,3:T(8,128)(2,1)} %bitcast.170), kind=kOutput, calls=%fused_computation.14 | convolution fusion | flops 805306368 | bytes 6553600 | tf_op jit(solution)/shard_map/sgpqe,dge->spqd/dot_general | solution.py:153
  328.3 34.1 %reduce-scatter.5.cloned.1.call-done = f32[1,4,16,3072]{3,2,1,0:T(8,128)} async-done(((f32[4,4,16,3072]{3,2,1,0:T(8,128)}), f32[1,4,16,3072]{3,2,1,0:T(8,128)}) %reduce-scatter.5.cloned.1.call-update) | async-done | bytes 786448 | tf_op jit(solution)/shard_map/reduce_scatter | solution.py:152
  364.5 22.1 %all-gather.1 = f32[32,16,64]{2,1,0:T(8,128)S(1)} all-gather(f32[4,16,64]{2,1,0:T(8,128)S(1)} %fusion.63), channel_id=3, replica_groups=mesh['section'=2,'seq'=32,'cfg'=4] {'section','cfg'}, dimensions={0}, use_global_device_ids=true | all-gather | bytes 147456 | tf_op jit(solution)/shard_map/all_gather | solution.py:170
  386.6 2.5 fusion.75
  (175 shorter events, 52.0 us)
Async XLA Ops:
  8.0 356.1 %copy-start = (bf16[3072,64]{0,1:T(8,128)(2,1)S(1)}, bf16[3072,64]{0,1:T(8,128)(2,1)}, u32[]{:S(2)}) copy-start(bf16[3072,64]{0,1:T(8,128)(2,1)} %param.19) | copy-start | bytes 1179652
  8.0 39.1 %all-gather.6.cloned.1.call-start = ((), (), s32[]{:S(2)}) async-start(), calls=%async_computation.6 | async-start | bytes 1966080 | tf_op jit(solution)/shard_map/all_gather | solution.py:120
  8.1 18.7 %copy-start.22 = (pred[4,16]{1,0:T(4,128)(4,1)}, pred[4,16]{1,0:T(4,128)(4,1)S(1)}, u32[]{:S(2)}) copy-start(pred[4,16]{1,0:T(4,128)(4,1)S(1)} %add_compare_fusion.1) | copy-start | bytes 196
  62.9 30.6 %all-to-all-start = ((bf16[32,3,4,1024]{3,2,1,0:T(4,128)(2,1)}), bf16[32,3,4,1024]{3,2,1,0:T(4,128)(2,1)S(1)}, u32[]{:S(2)}, u32[]{:S(2)}) async-start(bf16[32,3,4,1024]{3,2,1,0:T(4,128)(2,1)} %copy.44), calls=%async_computation | async-start | bytes 1572864 | tf_op jit(solution)/shard_map/all_to_all | solution.py:128
  72.4 79.6 %all-gather.10.cloned.1.call-start = ((), (), s32[]{:S(2)}) async-start(), calls=%async_computation.10 | async-start | bytes 3244032 | tf_op jit(solution)/shard_map/all_gather | solution.py:89
  73.0 129.8 %reduce-scatter.3.cloned.1.call-start = ((), (), s32[]{:S(2)}) async-start(), calls=%async_computation.7 | async-start | bytes 3932160 | tf_op jit(solution)/shard_map/reduce_scatter | solution.py:152
  124.2 78.7 %copy-start.1 = (bf16[1,4,16,3072]{3,2,1,0:T(8,128)(2,1)S(1)}, bf16[1,4,16,3072]{3,2,1,0:T(8,128)(2,1)}, u32[]{:S(2)}) copy-start(bf16[1,4,16,3072]{3,2,1,0:T(8,128)(2,1)} %param.12) | copy-start | bytes 1179652
  124.2 78.6 %copy-start.10 = (f32[1,1,3072]{2,0,1:T(1,128)S(1)}, f32[1,1,3072]{2,0,1:T(1,128)}, u32[]{:S(2)}) copy-start(f32[1,1,3072]{2,0,1:T(1,128)} %get-tuple-element.35) | copy-start | bytes 36868
  124.2 78.6 %copy-start.23 = (pred[4,16]{1,0:T(4,128)(4,1)S(1)}, pred[4,16]{1,0:T(4,128)(4,1)}, u32[]{:S(2)}) copy-start(pred[4,16]{1,0:T(4,128)(4,1)} %copy-done.22) | copy-start | bytes 196
  124.2 82.4 %copy-start.12 = (f32[1,1,3072]{2,0,1:T(1,128)S(1)}, f32[1,1,3072]{2,0,1:T(1,128)}, u32[]{:S(2)}) copy-start(f32[1,1,3072]{2,0,1:T(1,128)} %copy-done.11) | copy-start | bytes 36868
  124.2 82.4 %copy-start.14 = (f32[1,1,3072]{2,0,1:T(1,128)S(1)}, f32[1,1,3072]{2,0,1:T(1,128)}, u32[]{:S(2)}) copy-start(f32[1,1,3072]{2,0,1:T(1,128)} %copy-done.13) | copy-start | bytes 36868
  124.2 82.4 %copy-start.16 = (f32[1,1,3072]{2,0,1:T(1,128)S(1)}, f32[1,1,3072]{2,0,1:T(1,128)}, u32[]{:S(2)}) copy-start(f32[1,1,3072]{2,0,1:T(1,128)} %copy-done.15) | copy-start | bytes 36868
  124.2 82.4 %copy-start.18 = (f32[1,1,3072]{2,0,1:T(1,128)S(1)}, f32[1,1,3072]{2,0,1:T(1,128)}, u32[]{:S(2)}) copy-start(f32[1,1,3072]{2,0,1:T(1,128)} %copy-done.17) | copy-start | bytes 36868
  161.2 75.2 %all-gather.8.cloned.1.call-start = ((), (), s32[]{:S(2)}) async-start(), calls=%async_computation.8 | async-start | bytes 1966080 | tf_op jit(solution)/shard_map/all_gather | solution.py:120
  204.2 2.1 collective-permute-start
  207.7 154.7 %reduce-scatter.5.cloned.1.call-start = ((), (), s32[]{:S(2)}) async-start(), calls=%async_computation.9 | async-start | bytes 3932160 | tf_op jit(solution)/shard_map/reduce_scatter | solution.py:152
  250.1 36.6 %copy-start.19 = (pred[4,2048]{1,0:T(4,128)(4,1)S(1)}, pred[4,2048]{1,0:T(4,128)(4,1)}, u32[]{:S(2)}) copy-start(pred[4,2048]{1,0:T(4,128)(4,1)} %iota_compare_fusion) | copy-start | bytes 24580
  302.0 22.9 %copy-start.25 = (f32[1,3]{1,0:T(1,128)S(1)}, f32[1,3]{1,0:T(1,128)}, u32[]{:S(2)}) copy-start(f32[1,3]{1,0:T(1,128)} %param.20) | copy-start | bytes 40
  302.0 23.5 %copy-start.21 = (f32[2,3072]{1,0:T(2,128)S(1)}, f32[2,3072]{1,0:T(2,128)}, u32[]{:S(2)}) copy-start(f32[2,3072]{1,0:T(2,128)} %param.18) | copy-start | bytes 73732
  302.0 23.5 %copy-start.3 = (bf16[1,1,4,32,1024]{4,3,2,1,0:T(8,128)(2,1)S(1)}, bf16[1,1,4,32,1024]{4,3,2,1,0:T(8,128)(2,1)}, u32[]{:S(2)}) copy-start(bf16[1,1,4,32,1024]{4,3,2,1,0:T(8,128)(2,1)} %copy-done.2) | copy-start | bytes 786436
  302.0 23.9 %copy-start.5 = (bf16[1,1,4,32,1024]{4,3,2,1,0:T(8,128)(2,1)S(1)}, bf16[1,1,4,32,1024]{4,3,2,1,0:T(8,128)(2,1)}, u32[]{:S(2)}) copy-start(bf16[1,1,4,32,1024]{4,3,2,1,0:T(8,128)(2,1)} %copy-done.4) | copy-start | bytes 786436
  302.0 24.3 %copy-start.7 = (bf16[1,1,4,32,1024]{4,3,2,1,0:T(8,128)(2,1)S(1)}, bf16[1,1,4,32,1024]{4,3,2,1,0:T(8,128)(2,1)}, u32[]{:S(2)}) copy-start(bf16[1,1,4,32,1024]{4,3,2,1,0:T(8,128)(2,1)} %copy-done.6) | copy-start | bytes 786436
  302.0 24.6 %copy-start.9 = (bf16[1,1,4,32,1024]{4,3,2,1,0:T(8,128)(2,1)S(1)}, bf16[1,1,4,32,1024]{4,3,2,1,0:T(8,128)(2,1)}, u32[]{:S(2)}) copy-start(bf16[1,1,4,32,1024]{4,3,2,1,0:T(8,128)(2,1)} %copy-done.8) | copy-start | bytes 786436
  324.8 61.8 %copy-start.20 = (f32[1,4,16,64]{3,2,1,0:T(8,128)S(1)}, f32[1,4,16,64]{3,2,1,0:T(8,128)}, u32[]{:S(2)}) copy-start(f32[1,4,16,64]{3,2,1,0:T(8,128)} %param.13) | copy-start | bytes 49156
  (11 other events, 58.1 us)
Sparse Core Ops, SparseCore 0:
  14.2 32.8 all-gather.5
  161.4 41.4 reduce-scatter.2
  207.8 28.5 all-gather.7
  324.9 37.3 reduce-scatter.4
Sparse Core Ops, SparseCore 1:
  75.5 76.5 all-gather.9
where the time goes:
time: 404 us; the launch traced here: 396 us
  waiting for transfers between devices  169 us (42%)
  blocking collectives  84.7 us (21%)
  local copies, waits for them, and re-layouts  39.7 us (10%)
  matrix products  39.5 us (10%)
  other arithmetic  35.8 us (9%)
  between operations  16.5 us (4%)
  starting transfers between devices  11.1 us (3%)
    reduce_scatter x2, waiting for transfers between devices, run(): lax.psum_scatter(jnp.einsum('sgpqe,dge->spqd', returned, out_full, prefer...  75.6 us
    all_gather x2, waiting for transfers between devices, run(): mixed_rows = lax.all_gather(mixed_rows, 'cfg', axis=0, tiled=True)  48.4 us
    all_to_all x2, blocking collectives, run(): lax.all_to_all(attended, 'seq', split_axis=2, concat_axis=0, tiled=True)  32 us
    all_to_all x1, blocking collectives, run(): lax.all_to_all(outgoing, 'seq', split_axis=0, concat_axis=3, tiled=True)  30.6 us
    all_gather x1, waiting for transfers between devices, per_device(): lax.all_gather(out_weight[0], 'seq', axis=0, tiled=True)  27.8 us
    all_gather x1, blocking collectives, per_device(): lax.all_gather(predicted, ('section', 'cfg'), axis=0, tiled=True)  22.1 us
    dot_general x2, matrix products, run(): jnp.einsum('spqd,djge->sgjpqe', mixed_rows, qkv_full, preferred_element_t...  16.2 us
    all_to_all x1, waiting for transfers between devices, run(): lax.all_to_all(outgoing, 'seq', split_axis=0, concat_axis=3, tiled=True)  15.6 us
  transfers between devices with their start and end apart: 7, of which 7 were waited for; matrix products, arithmetic and copies ran while one was open for 9% of the time, Pallas kernels for 0%

commit v1 on v0

--- a/solution.py
+++ b/solution.py
@@ -3,6 +3,7 @@
 import jax.numpy as jnp
 from jax import lax
 from jax.sharding import PartitionSpec as P
+from jax.lax import all_to_all, axis_size
 
 HD = 64
 TEXT = 226
@@ -86,9 +87,9 @@
     group_heads = qkv_weight.shape[3] // HD
     seq_count = cfg_devices
     qkv_full = qkv_weight[0].reshape(width, 3, group_heads, HD)
-    out_full = lax.all_gather(out_weight[0], "seq", axis=0, tiled=True).reshape(
-        width, group_heads, HD
-    )
+    out_full = jnp.concatenate(
+        all_to_all(jnp.stack(axis_size("seq") * [out_weight[0]]), "seq", 0, 0), axis=0
+    ).reshape(width, group_heads, HD)
     mod_rows = modulation[0]
     stale_rows = stale_cache[0, 0, 0]
     my_sequence = shard_id // group_heads

time: 404 us -> 459 us (1.14)
  waiting for transfers between devices: 169 us -> 210 us
  local copies, waits for them, and re-layouts: 39.7 us -> 53 us
    all_to_all x0 -> x1, waiting for transfers between devices: none -> 66.6 us  [per_device(): all_to_all(jnp.stack(axis_size('seq') * [out_weight[0]]), 'seq', 0, 0)]
    all_gather x1 -> x0, waiting for transfers between devices: 27.8 us -> none  [per_device(): lax.all_gather(out_weight[0], 'seq', axis=0, tiled=True)]
    another operation x0 -> x2, local copies, waits for them, and re-layouts: none -> 10.6 us  [the longest x1 8.59 us: per_device(): out_full = jnp.concatenate(all_to_all(jnp.stack(axis_size('seq') * [out_w...]
    all_to_all x0 -> x1, local copies, waits for them, and re-layouts: none -> 5.72 us  [per_device(): all_to_all(jnp.stack(axis_size('seq') * [out_weight[0]]), 'seq', 0, 0)]
    all_gather x1 -> x0, local copies, waits for them, and re-layouts: 4.65 us -> none  [per_device(): lax.all_gather(out_weight[0], 'seq', axis=0, tiled=True)]
    unnamed x57 -> x75, local copies, waits for them, and re-layouts: 12.9 us -> 12.9 us
  transfers between devices with their start and end apart: 7 -> 7, of which waited for: 7 -> 7; matrix products, arithmetic and copies ran while one was open for 9% -> 5% of each run, Pallas kernels for 0% -> 0%
where the time goes in v1:
time: 459 us; the launch traced here: 451 us
  waiting for transfers between devices  210 us (46%)
  blocking collectives  84.7 us (18%)
  local copies, waits for them, and re-layouts  53 us (12%)
  matrix products  39 us (8%)
  other arithmetic  34.5 us (8%)
  starting transfers between devices  15.1 us (3%)
  between operations  15.1 us (3%)
    reduce_scatter x2, waiting for transfers between devices, run(): lax.psum_scatter(jnp.einsum('sgpqe,dge->spqd', returned, out_full, prefer...  74.9 us
    all_to_all x1, waiting for transfers between devices, per_device(): all_to_all(jnp.stack(axis_size('seq') * [out_weight[0]]), 'seq', 0, 0)  66.6 us
    all_gather x2, waiting for transfers between devices, run(): mixed_rows = lax.all_gather(mixed_rows, 'cfg', axis=0, tiled=True)  48.5 us
    all_to_all x2, blocking collectives, run(): lax.all_to_all(attended, 'seq', split_axis=2, concat_axis=0, tiled=True)  32 us
    all_to_all x1, blocking collectives, run(): lax.all_to_all(outgoing, 'seq', split_axis=0, concat_axis=3, tiled=True)  30.6 us
    all_gather x1, blocking collectives, per_device(): lax.all_gather(predicted, ('section', 'cfg'), axis=0, tiled=True)  22.1 us
    all_to_all x1, waiting for transfers between devices, run(): lax.all_to_all(outgoing, 'seq', split_axis=0, concat_axis=3, tiled=True)  18.1 us
    dot_general x2, matrix products, run(): jnp.einsum('spqd,djge->sgjpqe', mixed_rows, qkv_full, preferred_element_t...  16.2 us
  transfers between devices with their start and end apart: 7, of which 7 were waited for; matrix products, arithmetic and copies ran while one was open for 5% of the time, Pallas kernels for 0%

profile of v1, /device:TPU:1, one launch (start us, length us, event | category | flops | bytes accessed | tf_op | source)
XLA Modules:
  0.0 451.0 jit_solution(5998155164784358680)
XLA Ops:
  13.3 12.7 %copy.39 = bf16[1,3072,3,512]{1,3,2,0:T(8,128)(2,1)} copy(bf16[1,3072,3,512]{3,1,2,0:T(8,128)(2,1)} %param.15) | data formatting | bytes 18874368 | tf_op args[3]
  26.4 19.9 %all-gather.4.cloned.1.call-done = bf16[4,4,16,3072]{3,2,1,0:T(8,128)(2,1)} async-done(((bf16[1,4,16,3072]{3,2,1,0:T(8,128)(2,1)}), bf16[4,4,16,3072]{3,2,1,0:T(8,128)(2,1)}) %all-gather.4.cloned.1.call-update) | async-done | bytes 1572880 | tf_op jit(solution)/shard_map/all_gather | solution.py:121
  46.3 8.1 %convolution_bitcast_fusion.3 = f32[4,8,3,4,16,64]{5,4,1,2,3,0:T(8,128)S(1)} fusion(bf16[3072,3,8,64,1,1]{0,3,2,1,5,4:T(8,128)(2,1)} %bitcast.168, bf16[4,4,16,3072]{3,2,1,0:T(8,128)(2,1)} %all-gather.4.cloned.1.call-done), kind=kOutput, calls=%fused_computation.21 | convolution fusion | flops 2415919104 | bytes 12582912 | tf_op jit(solution)/shard_map/spqd,djge->sgjpqe/dot_general | solution.py:122
  62.2 10.0 %all-to-all-start = ((bf16[32,3,4,1024]{3,2,1,0:T(4,128)(2,1)}), bf16[32,3,4,1024]{3,2,1,0:T(4,128)(2,1)S(1)}, u32[]{:S(2)}, u32[]{:S(2)}) async-start(bf16[32,3,4,1024]{3,2,1,0:T(4,128)(2,1)} %copy.44), calls=%async_computation | async-start | bytes 1572864 | tf_op jit(solution)/shard_map/all_to_all | solution.py:129
  75.1 18.1 %all-to-all-done = bf16[32,3,4,1024]{3,2,1,0:T(4,128)(2,1)S(1)} async-done(((bf16[32,3,4,1024]{3,2,1,0:T(4,128)(2,1)}), bf16[32,3,4,1024]{3,2,1,0:T(4,128)(2,1)S(1)}, u32[]{:S(2)}, u32[]{:S(2)}) %all-to-all-start) | async-done | bytes 786464 | tf_op jit(solution)/shard_map/all_to_all | solution.py:129
  98.2 3.7 fusion.2
  101.9 4.0 fusion.27
  106.8 16.1 %all_to_all.65 = bf16[1,4,32,1024]{3,1,0,2:T(4,128)(2,1)} all-to-all(bf16[1,4,32,1024]{3,1,0,2:T(4,128)(2,1)S(1)} %copy.52), channel_id=1, replica_groups=mesh['section'=2,'seq'=32,'cfg'=4] {'seq'}, dimensions={2} | all-to-all | bytes 524288 | tf_op jit(solution)/shard_map/all_to_all | solution.py:151
  124.9 4.1 all-to-all-start.2
  131.1 66.6 %all-to-all-done.2 = bf16[32,96,512]{2,1,0:T(8,128)(2,1)S(1)} async-done(((bf16[32,96,512]{2,1,0:T(8,128)(2,1)}), bf16[32,96,512]{2,1,0:T(8,128)(2,1)S(1)}, u32[]{:S(2)}, u32[]{:S(2)}) %all-to-all-start.2) | async-done | bytes 3145760 | tf_op jit(solution)/shard_map/all_to_all | solution.py:91
  197.7 5.7 %copy.54 = bf16[32,96,512]{1,0,2:T(8,128)(2,1)} copy(bf16[32,96,512]{2,1,0:T(8,128)(2,1)S(1)} %all-to-all-done.2) | data formatting | bytes 6291456 | tf_op jit(solution)/shard_map/all_to_all | solution.py:91
  203.4 8.6 %reshape.443 = bf16[3072,8,64,1,1]{0,2,1,3,4:T(8,128)(2,1)} reshape(bf16[32,96,512]{1,0,2:T(8,128)(2,1)} %copy.54) | data formatting | bytes 6291456 | tf_op jit(solution)/shard_map/reshape;reshape | solution.py:92
  212.0 4.8 %convolution_bitcast_fusion.1 = f32[4,4,16,3072]{3,2,1,0:T(8,128)} fusion(bf16[4,8,4,16,64]{4,3,2,1,0:T(8,128)(2,1)} %reshape.448, bf16[3072,8,64,1,1]{0,2,1,3,4:T(8,128)(2,1)} %reshape.443), kind=kOutput, calls=%fused_computation.15 | convolution fusion | flops 805306368 | bytes 6553600 | tf_op jit(solution)/shard_map/sgpqe,dge->spqd/dot_general | solution.py:154
  217.1 40.8 %reduce-scatter.3.cloned.1.call-done = f32[1,4,16,3072]{3,2,1,0:T(8,128)} async-done(((f32[4,4,16,3072]{3,2,1,0:T(8,128)}), f32[1,4,16,3072]{3,2,1,0:T(8,128)}) %reduce-scatter.3.cloned.1.call-update) | async-done | bytes 786448 | tf_op jit(solution)/shard_map/reduce_scatter | solution.py:153
  262.8 28.7 %all-gather.6.cloned.1.call-done = bf16[4,4,16,3072]{3,2,1,0:T(8,128)(2,1)} async-done(((bf16[1,4,16,3072]{3,2,1,0:T(8,128)(2,1)}), bf16[4,4,16,3072]{3,2,1,0:T(8,128)(2,1)}) %all-gather.6.cloned.1.call-update) | async-done | bytes 1572880 | tf_op jit(solution)/shard_map/all_gather | solution.py:121
  291.4 8.1 %convolution_bitcast_fusion.2 = f32[4,8,3,4,16,64]{5,4,1,3,0,2:T(8,128)S(1)} fusion(bf16[3072,3,8,64,1,1]{0,3,2,5,4,1:T(8,128)(2,1)} %bitcast.169, bf16[4,4,16,3072]{3,2,1,0:T(8,128)(2,1)} %all-gather.6.cloned.1.call-done), kind=kOutput, calls=%fused_computation.20 | convolution fusion | flops 2415919104 | bytes 12582912 | tf_op jit(solution)/shard_map/spqd,djge->sgjpqe/dot_general | solution.py:122
  309.8 30.6 %all_to_all.66 = bf16[32,3,4,1024]{3,2,1,0:T(4,128)(2,1)S(1)} all-to-all(bf16[32,3,4,1024]{3,2,1,0:T(4,128)(2,1)S(1)} %copy.60), channel_id=1, replica_groups=mesh['section'=2,'seq'=32,'cfg'=4] {'seq'}, dimensions={0} | all-to-all | bytes 1572864 | tf_op jit(solution)/shard_map/all_to_all | solution.py:129
  348.0 2.5 fusion.1
  350.5 3.7 fusion.4
  354.2 4.0 fusion.37
  359.2 16.0 %all_to_all.67 = bf16[1,4,32,1024]{3,1,0,2:T(4,128)(2,1)S(1)} all-to-all(bf16[1,4,32,1024]{3,1,0,2:T(4,128)(2,1)S(1)} %copy.67), channel_id=1, replica_groups=mesh['section'=2,'seq'=32,'cfg'=4] {'seq'}, dimensions={2} | all-to-all | bytes 524288 | tf_op jit(solution)/shard_map/all_to_all | solution.py:151
  375.5 4.6 %convolution_bitcast_fusion = f32[4,4,16,3072]{3,2,1,0:T(8,128)} fusion(bf16[4,8,4,16,64]{4,3,2,1,0:T(8,128)(2,1)S(1)} %reshape.450, bf16[3072,8,64,1,1]{0,2,1,3,4:T(8,128)(2,1)} %reshape.443), kind=kOutput, calls=%fused_computation.14 | convolution fusion | flops 805306368 | bytes 6553600 | tf_op jit(solution)/shard_map/sgpqe,dge->spqd/dot_general | solution.py:154
  383.5 34.1 %reduce-scatter.5.cloned.1.call-done = f32[1,4,16,3072]{3,2,1,0:T(8,128)} async-done(((f32[4,4,16,3072]{3,2,1,0:T(8,128)}), f32[1,4,16,3072]{3,2,1,0:T(8,128)}) %reduce-scatter.5.cloned.1.call-update) | async-done | bytes 786448 | tf_op jit(solution)/shard_map/reduce_scatter | solution.py:153
  419.7 22.1 %all-gather = f32[32,16,64]{2,1,0:T(8,128)S(1)} all-gather(f32[4,16,64]{2,1,0:T(8,128)S(1)} %fusion.65), channel_id=2, replica_groups=mesh['section'=2,'seq'=32,'cfg'=4] {'section','cfg'}, dimensions={0}, use_global_device_ids=true | all-gather | bytes 147456 | tf_op jit(solution)/shard_map/all_gather | solution.py:171
  (194 shorter events, 58.3 us)
Async XLA Ops:
  7.2 412.2 %copy-start = (bf16[3072,64]{0,1:T(8,128)(2,1)S(1)}, bf16[3072,64]{0,1:T(8,128)(2,1)}, u32[]{:S(2)}) copy-start(bf16[3072,64]{0,1:T(8,128)(2,1)} %param.19) | copy-start | bytes 1179652
  7.2 39.1 %all-gather.4.cloned.1.call-start = ((), (), s32[]{:S(2)}) async-start(), calls=%async_computation.7 | async-start | bytes 1966080 | tf_op jit(solution)/shard_map/all_gather | solution.py:121
  62.2 31.1 %all-to-all-start = ((bf16[32,3,4,1024]{3,2,1,0:T(4,128)(2,1)}), bf16[32,3,4,1024]{3,2,1,0:T(4,128)(2,1)S(1)}, u32[]{:S(2)}, u32[]{:S(2)}) async-start(bf16[32,3,4,1024]{3,2,1,0:T(4,128)(2,1)} %copy.44), calls=%async_computation | async-start | bytes 1572864 | tf_op jit(solution)/shard_map/all_to_all | solution.py:129
  72.4 25.8 %copy-start.2 = (bf16[2048,128]{0,1:T(8,128)(2,1)}, bf16[2048,128]{0,1:T(8,128)(2,1)S(1)}, u32[]{:S(2)}) copy-start(bf16[2048,128]{0,1:T(8,128)(2,1)S(1)} %copy.49) | copy-start | bytes 1572868
  75.1 23.1 %copy-start.27 = (pred[4,2048]{1,0:T(4,128)(4,1)}, pred[4,2048]{1,0:T(4,128)(4,1)S(1)}, u32[]{:S(2)}) copy-start(pred[4,2048]{1,0:T(4,128)(4,1)S(1)} %iota_compare_fusion) | copy-start | bytes 24580
  124.9 72.8 %all-to-all-start.2 = ((bf16[32,96,512]{2,1,0:T(8,128)(2,1)}), bf16[32,96,512]{2,1,0:T(8,128)(2,1)S(1)}, u32[]{:S(2)}, u32[]{:S(2)}) async-start(bf16[32,96,512]{2,1,0:T(8,128)(2,1)} %stack.29), calls=%async_computation.2 | async-start | bytes 6291456 | tf_op jit(solution)/shard_map/all_to_all | solution.py:91
  129.0 128.9 %reduce-scatter.3.cloned.1.call-start = ((), (), s32[]{:S(2)}) async-start(), calls=%async_computation.8 | async-start | bytes 3932160 | tf_op jit(solution)/shard_map/reduce_scatter | solution.py:153
  203.4 54.4 %copy-start.1 = (bf16[1,4,16,3072]{3,2,1,0:T(8,128)(2,1)S(1)}, bf16[1,4,16,3072]{3,2,1,0:T(8,128)(2,1)}, u32[]{:S(2)}) copy-start(bf16[1,4,16,3072]{3,2,1,0:T(8,128)(2,1)} %param.12) | copy-start | bytes 1179652
  203.4 54.4 %copy-start.17 = (f32[1,1,3072]{2,0,1:T(1,128)S(1)}, f32[1,1,3072]{2,0,1:T(1,128)}, u32[]{:S(2)}) copy-start(f32[1,1,3072]{2,0,1:T(1,128)} %get-tuple-element.35) | copy-start | bytes 36868
  203.4 54.4 %copy-start.32 = (pred[4,16]{1,0:T(4,128)(4,1)S(1)}, pred[4,16]{1,0:T(4,128)(4,1)}, u32[]{:S(2)}) copy-start(pred[4,16]{1,0:T(4,128)(4,1)} %copy-done.31) | copy-start | bytes 196
  212.0 49.6 %copy-start.19 = (f32[1,1,3072]{2,0,1:T(1,128)S(1)}, f32[1,1,3072]{2,0,1:T(1,128)}, u32[]{:S(2)}) copy-start(f32[1,1,3072]{2,0,1:T(1,128)} %copy-done.18) | copy-start | bytes 36868
  212.0 49.6 %copy-start.21 = (f32[1,1,3072]{2,0,1:T(1,128)S(1)}, f32[1,1,3072]{2,0,1:T(1,128)}, u32[]{:S(2)}) copy-start(f32[1,1,3072]{2,0,1:T(1,128)} %copy-done.20) | copy-start | bytes 36868
  212.0 49.6 %copy-start.23 = (f32[1,1,3072]{2,0,1:T(1,128)S(1)}, f32[1,1,3072]{2,0,1:T(1,128)}, u32[]{:S(2)}) copy-start(f32[1,1,3072]{2,0,1:T(1,128)} %copy-done.22) | copy-start | bytes 36868
  212.0 49.6 %copy-start.25 = (f32[1,1,3072]{2,0,1:T(1,128)S(1)}, f32[1,1,3072]{2,0,1:T(1,128)}, u32[]{:S(2)}) copy-start(f32[1,1,3072]{2,0,1:T(1,128)} %copy-done.24) | copy-start | bytes 36868
  216.8 74.6 %all-gather.6.cloned.1.call-start = ((), (), s32[]{:S(2)}) async-start(), calls=%async_computation.9 | async-start | bytes 1966080 | tf_op jit(solution)/shard_map/all_gather | solution.py:121
  259.2 2.1 collective-permute-start
  262.7 154.9 %reduce-scatter.5.cloned.1.call-start = ((), (), s32[]{:S(2)}) async-start(), calls=%async_computation.10 | async-start | bytes 3932160 | tf_op jit(solution)/shard_map/reduce_scatter | solution.py:153
  306.0 37.6 %copy-start.3 = (bf16[2048,128]{0,1:T(8,128)(2,1)S(1)}, bf16[2048,128]{0,1:T(8,128)(2,1)}, u32[]{:S(2)}) copy-start(bf16[2048,128]{0,1:T(8,128)(2,1)} %copy-done.2) | copy-start | bytes 1572868
  306.0 37.6 %copy-start.28 = (pred[4,2048]{1,0:T(4,128)(4,1)S(1)}, pred[4,2048]{1,0:T(4,128)(4,1)}, u32[]{:S(2)}) copy-start(pred[4,2048]{1,0:T(4,128)(4,1)} %copy-done.27) | copy-start | bytes 24580
  358.3 22.4 %copy-start.5 = (bf16[1,1,4,32,1024]{4,3,2,1,0:T(8,128)(2,1)S(1)}, bf16[1,1,4,32,1024]{4,3,2,1,0:T(8,128)(2,1)}, u32[]{:S(2)}) copy-start(bf16[1,1,4,32,1024]{4,3,2,1,0:T(8,128)(2,1)} %copy-done.4) | copy-start | bytes 786436
  358.3 22.8 %copy-start.7 = (bf16[1,1,4,32,1024]{4,3,2,1,0:T(8,128)(2,1)S(1)}, bf16[1,1,4,32,1024]{4,3,2,1,0:T(8,128)(2,1)}, u32[]{:S(2)}) copy-start(bf16[1,1,4,32,1024]{4,3,2,1,0:T(8,128)(2,1)} %copy-done.6) | copy-start | bytes 786436
  358.3 23.1 %copy-start.9 = (bf16[1,1,4,32,1024]{4,3,2,1,0:T(8,128)(2,1)S(1)}, bf16[1,1,4,32,1024]{4,3,2,1,0:T(8,128)(2,1)}, u32[]{:S(2)}) copy-start(bf16[1,1,4,32,1024]{4,3,2,1,0:T(8,128)(2,1)} %copy-done.8) | copy-start | bytes 786436
  358.3 23.5 %copy-start.11 = (bf16[1,1,4,32,1024]{4,3,2,1,0:T(8,128)(2,1)S(1)}, bf16[1,1,4,32,1024]{4,3,2,1,0:T(8,128)(2,1)}, u32[]{:S(2)}) copy-start(bf16[1,1,4,32,1024]{4,3,2,1,0:T(8,128)(2,1)} %copy-done.10) | copy-start | bytes 786436
  380.1 61.7 %copy-start.29 = (f32[1,4,16,64]{3,2,1,0:T(8,128)S(1)}, f32[1,4,16,64]{3,2,1,0:T(8,128)}, u32[]{:S(2)}) copy-start(f32[1,4,16,64]{3,2,1,0:T(8,128)} %param.13) | copy-start | bytes 49156
  (20 other events, 163.8 us)
Sparse Core Ops, SparseCore 0:
  13.4 32.8 all-gather.3
  217.0 40.8 reduce-scatter.2
  262.9 28.5 all-gather.5
  380.2 37.3 reduce-scatter.4
